TPU v7x, 32 devices: a whole 2x2x4 slice. The times are simulated.
32 devices in a mesh: section: 2 (over x), fsdp: 4 (over z), dp: 4 (over y, core).
Axes of the slice: x: 2, y: 2, z: 4, core: 2. Of those that a mesh axis runs over, the one named last changes fastest.
Arguments:
- activations: bfloat16 [2, 4, 512, 3584], P('section', None, ('fsdp', 'dp')), may hold values from -6 to 6
- out_grad: bfloat16 [2, 4, 512, 14336], P('section', None, ('fsdp', 'dp')), may hold values from -6 to 6
- blocks: bfloat16 [2, 16, 128, 128], P('section', 'fsdp'), may hold values from -0.5 to 0.5
- pattern: int32 [2, 16, 2], P('section', 'fsdp'), may hold values from 0 to 111, as said below
- order: int32 [4], replicated, may hold values from 0 to 3, each once
Outputs:
- received: bfloat16 [2, 4, 512, 3584], P('section', None, ('fsdp', 'dp'))
- weight_grad: float32 [2, 16, 128, 128], P('section', 'fsdp')
Inputs may be any that keep to these rules, and one draw needn't show every extreme that they name: pattern[s, b, 0] < 28 and pattern[s, b, 1] < 112; no two blocks of one section share both indices; within a section the blocks stand in ascending order of (row, column). `order`: a permutation of the microbatches.
All inputs are finite; a program needn't handle non-finite values.
Results may differ from a plain program's by a relative error of at most 0.0049.
Values may be sent and summed in bfloat16 or wider, within the bound.
No kernel may reach another device: no remote copies, remote signals or barrier semaphores. Data moves between devices by JAX's collectives and lax.ppermute only.
A program may use at most 128 MiB of HBM per device.

v0:
```python
import math
import jax
import jax.numpy as jnp
from jax import lax
from jax.sharding import PartitionSpec as P


def passed_along(block, axis, distance):
    devices = range(lax.axis_size(axis))
    route = [(i - distance, i) for i in devices if i - distance in devices]
    return lax.ppermute(block, axis, route)


def silu_slope(pre_act):
    sigmoid_val = jax.nn.sigmoid(pre_act)
    return sigmoid_val * (1.0 + pre_act * (1.0 - sigmoid_val))


def in_groups(step_fn, running, shard_blocks, first_block):
    block_count = shard_blocks.shape[0]
    group_size = math.gcd(block_count, 32)
    if group_size == block_count:
        return step_fn(running, shard_blocks, first_block)

    def one_group(number, carried):
        segment = lax.dynamic_slice_in_dim(shard_blocks, number * group_size, group_size, 0)
        return step_fn(carried, segment, first_block + number * group_size)

    return lax.fori_loop(0, block_count // group_size, one_group, running)


def local(activations, out_grad, blocks, pattern, order):
    block_size = blocks.shape[-1]
    micro_count = activations.shape[1]
    tok_rows = activations.shape[1] * activations.shape[2]
    row_count = activations.shape[3] // block_size
    col_count = out_grad.shape[3] // block_size
    features = activations[0].reshape(tok_rows, row_count, block_size)
    hidden_grad = out_grad[0].reshape(tok_rows, out_grad.shape[3])
    own_blocks = blocks[0]
    all_indices = lax.all_gather(pattern[0], "fsdp", axis=0, tiled=True)

    def forward_step(running, shard_blocks, first_block):
        indices = lax.dynamic_slice_in_dim(all_indices, first_block, shard_blocks.shape[0], 0)
        rows_in = jnp.take(features, indices[:, 0], axis=1)
        product = jnp.einsum(
            "tbk,bkn->tbn", rows_in, shard_blocks, preferred_element_type=jnp.float32
        )
        return running.at[:, indices[:, 1]].add(product)

    pre_zero = jnp.zeros((tok_rows, col_count, block_size), jnp.float32)
    pre_act = in_groups(
        forward_step, pre_zero, lax.all_gather(own_blocks, "fsdp", axis=0, tiled=True), jnp.int32(0)
    )
    act_grad = (hidden_grad.astype(jnp.float32) * silu_slope(pre_act.reshape(tok_rows, -1))).astype(
        jnp.bfloat16
    )
    grad_cols = act_grad.reshape(tok_rows, col_count, block_size)

    def backward_step(running, shard_blocks, first_block):
        indices = lax.dynamic_slice_in_dim(all_indices, first_block, shard_blocks.shape[0], 0)
        cols_in = jnp.take(grad_cols, indices[:, 1], axis=1)
        product = jnp.einsum(
            "tbn,bkn->tbk", cols_in, shard_blocks, preferred_element_type=jnp.float32
        )
        return running.at[:, indices[:, 0]].add(product)

    back_zero = jnp.zeros((tok_rows, row_count, block_size), jnp.float32)
    input_grad = in_groups(
        backward_step,
        back_zero,
        lax.all_gather(own_blocks, "fsdp", axis=0, tiled=True),
        jnp.int32(0),
    )
    input_grad = input_grad.astype(jnp.bfloat16).reshape(
        micro_count, activations.shape[2], activations.shape[3]
    )
    ordered = jnp.take(input_grad, order, axis=0)
    received = passed_along(ordered, "section", -1)
    indices = all_indices
    rows_in = jnp.take(features, indices[:, 0], axis=1)
    cols_in = jnp.take(grad_cols, indices[:, 1], axis=1)
    owned_grads = lax.psum_scatter(
        jnp.einsum("tbk,tbn->bkn", rows_in, cols_in, preferred_element_type=jnp.float32),
        "fsdp",
        scatter_dimension=0,
        tiled=True,
    )
    summed = lax.psum(owned_grads, "dp")
    grad_scale = 1.0 / math.sqrt(tok_rows * lax.axis_size("fsdp") * lax.axis_size("dp"))
    return (received[None], (summed * grad_scale)[None])


def solution(mesh):
    in_specs = (
        P("section", None, ("fsdp", "dp"), None),
        P("section", None, ("fsdp", "dp"), None),
        P("section", "fsdp", None, None),
        P("section", "fsdp", None),
        P(),
    )
    out_specs = (P("section", None, ("fsdp", "dp"), None), P("section", "fsdp", None, None))
    return jax.shard_map(local, mesh=mesh, in_specs=in_specs, out_specs=out_specs, check_vma=False)
```

profile of v0, /device:TPU:0, one launch (start us, length us, event | category | flops | bytes accessed | tf_op | source)
XLA Modules:
  0.0 135.6 jit_solution(16365849403868641486)
XLA Ops:
  7.2 0.0 reduce-scatter.2.cloned.1.call-start
  7.2 0.8 copy.12
  8.0 13.6 %all-gather = s32[1,16,2]{2,0,1:T(1,128)S(1)} all-gather(s32[1,4,2]{2,0,1:T(1,128)S(1)} %copy.12), channel_id=2, replica_groups=mesh['section'=2,'fsdp'=4,'dp'=4] {'fsdp'}, dimensions={1}, use_global_device_ids=true | all-gather | bytes 160 | tf_op jit(solution)/shard_map/all_gather | solution.py:41
  21.6 0.1 copy.13
  21.7 1.6 %reshape_squeeze.4 = bf16[128,28,128]{2,1,0:T(8,128)(2,1)S(1)} reshape(bf16[1,4,32,3584]{3,2,1,0:T(8,128)(2,1)} %param.9) | data formatting | bytes 1835008 | tf_op jit(solution)/shard_map/reshape;squeeze | solution.py:38
  23.3 0.4 copy.14
  23.7 16.1 %all-gather.1 = bf16[1,16,128,128]{3,2,0,1:T(8,128)(2,1)S(1)} all-gather(bf16[1,4,128,128]{3,2,0,1:T(8,128)(2,1)} %bitcast.40), channel_id=3, replica_groups=mesh['section'=2,'fsdp'=4,'dp'=4] {'fsdp'}, dimensions={1}, use_global_device_ids=true | all-gather | bytes 655360 | tf_op jit(solution)/shard_map/all_gather | solution.py:72
  39.8 5.9 %copy.20 = f32[16,8,112,128]{3,2,1,0:T(8,128)} copy(bf16[16,8,112,128]{3,1,2,0:T(8,128)(2,1)} %bitcast.38) | data formatting | bytes 11010048
  45.7 0.6 gather_fusion.1
  46.3 0.4 fusion.6
  46.7 3.9 %broadcast_in_dim.46 = f32[128,112,128]{2,0,1:T(8,128)} broadcast(f32[]{:T(128)} %constant.23.clone.1), dimensions={} | broadcast | bytes 7340036 | tf_op jit(solution)/shard_map/broadcast_in_dim | solution.py:51
  50.6 3.4 %scatter_fusion = f32[128,112,128]{2,0,1:T(8,128)} fusion(f32[128,112,128]{2,0,1:T(8,128)} %broadcast_in_dim.46, s32[16]{0:T(128)S(1)} %get-tuple-element.10, f32[16,128,128]{2,1,0:T(8,128)S(1)} %fusion.6), kind=kCustom, calls=%fused_computation.3 | custom fusion | flops 262144 | bytes 3145792 | tf_op jit(solution)/shard_map/scatter-add | solution.py:49
  54.0 8.4 %fusion = bf16[128,112,128]{2,0,1:T(8,128)(2,1)} fusion(f32[128,112,128]{2,1,0:T(8,128)} %bitcast.37, f32[128,112,128]{2,0,1:T(8,128)} %scatter_fusion), kind=kLoop, calls=%fused_computation.6 | loop fusion | flops 16515072 | bytes 18350080 | tf_op jit(solution)/shard_map/convert_element_type | solution.py:55
  62.4 2.7 %gather_fusion.2 = bf16[16,128,128]{2,1,0:T(8,128)(2,1)S(1)} fusion(bf16[128,112,128]{2,0,1:T(8,128)(2,1)} %fusion, s32[1024]{0:T(1024)S(1)} %get-tuple-element.12), kind=kCustom, calls=%fused_computation.1.clone | custom fusion | bytes 1048640 | tf_op jit(solution)/shard_map/jit(_take)/gather | solution.py:62
  65.1 1.4 %fusion.1 = f32[16,128,128]{2,1,0:T(8,128)} fusion(bf16[16,128,128]{2,1,0:T(8,128)(2,1)S(1)} %gather_fusion.1, pred[16]{0:T(512)(128)(4,1)S(1)} %get-tuple-element.8, bf16[16,128,128]{2,1,0:T(8,128)(2,1)S(1)} %gather_fusion.2, pred[16]{0:T(512)(128)(4,1)S(1)} %get-tuple-element.4), kind=kOutput, calls=%fused_computation.8 | convolution fusion | flops 67633152 | bytes 2097184 | tf_op jit(solution)/shard_map/tbk,tbn->bkn/dot_general | solution.py:84
  66.5 0.0 reduce-scatter.2.cloned.1.call-update
  66.6 0.0 all-reduce.2.cloned.1.call-start
  66.6 0.5 fusion.3
  67.2 0.2 broadcast_in_dim.45
  67.4 1.6 %scatter_fusion.1 = f32[128,28,128]{2,0,1:T(8,128)S(1)} fusion(f32[128,28,128]{2,0,1:T(8,128)S(1)} %broadcast_in_dim.45, s32[16]{0:T(128)S(1)} %get-tuple-element.11, f32[16,128,128]{2,1,0:T(8,128)S(1)} %fusion.3), kind=kCustom, calls=%fused_computation.4 | custom fusion | flops 262144 | bytes 3145792 | tf_op jit(solution)/shard_map/scatter-add | solution.py:66
  69.0 0.1 convert_element_type.17
  69.1 0.6 copy.17
  69.8 0.5 reshape.27
  70.3 0.6 gather_fusion
  70.9 0.2 broadcast_select_fusion
  71.1 1.3 collective-permute-start
  72.4 20.7 %reduce-scatter.2.cloned.1.call-done = f32[4,128,128]{2,1,0:T(8,128)} async-done(((f32[16,128,128]{2,1,0:T(8,128)}), f32[4,128,128]{2,1,0:T(8,128)}) %reduce-scatter.2.cloned.1.call-update) | async-done | bytes 262160 | tf_op jit(solution)/shard_map/reduce_scatter | solution.py:83
  93.0 0.0 all-reduce.2.cloned.1.call-update
  93.1 0.0 collective-permute-done
  93.1 33.1 %all-reduce.2.cloned.1.call-done = f32[4,128,128]{2,1,0:T(8,128)} async-done(((f32[4,128,128]{2,1,0:T(8,128)}), f32[4,128,128]{2,1,0:T(8,128)}) %all-reduce.2.cloned.1.call-update) | async-done | bytes 262160 | tf_op jit(solution)/shard_map/psum | solution.py:89
  126.2 1.7 %multiply_bitcast_fusion = f32[1,4,128,128]{3,2,1,0:T(8,128)} fusion(f32[4,128,128]{2,1,0:T(8,128)} %all-reduce.2.cloned.1.call-done), kind=kLoop, calls=%fused_computation.19 | loop fusion | flops 65536 | bytes 524288 | tf_op jit(solution)/shard_map/broadcast_in_dim | solution.py:91
  127.9 0.9 copy.28
  (8 shorter events, 0.0 us)
Async XLA Ops:
  7.2 85.9 %reduce-scatter.2.cloned.1.call-start = ((), (), s32[]{:S(2)}) async-start(), calls=%async_computation.1 | async-start | bytes 1310720 | tf_op jit(solution)/shard_map/reduce_scatter | solution.py:83
  54.0 13.1 %copy-start = (s32[4]{0:T(128)S(1)}, s32[4]{0:T(128)}, u32[]{:S(2)}) copy-start(s32[4]{0:T(128)} %param.13) | copy-start | bytes 52
  66.6 59.6 %all-reduce.2.cloned.1.call-start = ((), (), s32[]{:S(2)}) async-start(), calls=%async_computation.2 | async-start | bytes 524288 | tf_op jit(solution)/shard_map/psum | solution.py:89
  71.1 22.0 %collective-permute-start = (bf16[4,32,3584]{2,1,0:T(8,128)(2,1)S(1)}, bf16[4,32,3584]{2,1,0:T(8,128)(2,1)S(1)}, u32[]{:S(2)}, u32[]{:S(2)}) collective-permute-start(bf16[4,32,3584]{2,1,0:T(8,128)(2,1)S(1)} %broadcast_select_fusion), channel_id=1, source_target_pairs={{16,0},{17,1},{18,2},{19,3},{20,4},{21,5},{22,6},{23,7},{24,8},{25... | collective-permute-start | bytes 2752520 | tf_op jit(solution)/shard_map/ppermute | solution.py:11
Sparse Core Ops, SparseCore 0:
  66.7 26.2 reduce-scatter.1
  95.4 30.7 all-reduce.1
where the time goes:
time: 136 us
  waiting for transfers between devices  53.8 us (40%)
  blocking collectives  29.7 us (22%)
  local copies, waits for them, and re-layouts  18.8 us (14%)
  other arithmetic  15.4 us (11%)
  between operations  14.2 us (10%)
  matrix products  2.29 us (2%)
  starting transfers between devices  1.37 us (1%)
    psum x1, waiting for transfers between devices, local(): summed = lax.psum(owned_grads, 'dp')  33.1 us
    reduce_scatter x1, waiting for transfers between devices, local(): lax.psum_scatter(jnp.einsum('tbk,tbn->bkn', rows_in, cols_in, preferred_e...  20.7 us
    all_gather x1, blocking collectives, local(): lax.all_gather(own_blocks, 'fsdp', axis=0, tiled=True)  16.1 us
    all_gather x1, blocking collectives, local(): all_indices = lax.all_gather(pattern[0], 'fsdp', axis=0, tiled=True)  13.6 us
    convert_element_type x1, other arithmetic, local(): (hidden_grad.astype(jnp.float32) * silu_slope(pre_act.reshape(tok_rows, -...  8.43 us
    unnamed x5, local copies, waits for them, and re-layouts  7.54 us
    broadcast_in_dim x1, local copies, waits for them, and re-layouts, local(): pre_zero = jnp.zeros((tok_rows, col_count, block_size), jnp.float32)  3.95 us
    scatter-add x1, other arithmetic, forward_step(): return running.at[:, indices[:, 1]].add(product)  3.38 us
  transfers between devices with their start and end apart: 3, of which 2 were waited for; matrix products, arithmetic and copies ran while one was open for 3% of the time, Pallas kernels for 0%

commit v1 on v0

--- a/solution.py
+++ b/solution.py
@@ -3,6 +3,11 @@
 import jax.numpy as jnp
 from jax import lax
 from jax.sharding import PartitionSpec as P
+
+
+def gather_and_add(block, mesh_axis):
+    parts = lax.all_gather(block, mesh_axis)
+    return jnp.sum(parts, axis=0)
 
 
 def passed_along(block, axis, distance):
@@ -86,7 +91,7 @@
         scatter_dimension=0,
         tiled=True,
     )
-    summed = lax.psum(owned_grads, "dp")
+    summed = gather_and_add(owned_grads, "dp")
     grad_scale = 1.0 / math.sqrt(tok_rows * lax.axis_size("fsdp") * lax.axis_size("dp"))
     return (received[None], (summed * grad_scale)[None])
 

time: 136 us -> 127 us (0.934)
  waiting for transfers between devices: 53.8 us -> 44.5 us
    psum x1 -> x0, waiting for transfers between devices: 33.1 us -> none  [local(): summed = lax.psum(owned_grads, 'dp')]
    ppermute x1, waiting for transfers between devices: 0.01 us -> 22.3 us  [passed_along(): return lax.ppermute(block, axis, route)]
    broadcast_in_dim x1 -> x0, other arithmetic: 1.67 us -> none  [local(): return (received[None], (summed * grad_scale)[None])]
    reduce_scatter x1, waiting for transfers between devices: 20.7 us -> 22.1 us  [local(): lax.psum_scatter(jnp.einsum('tbk,tbn->bkn', rows_in, cols_in, preferred_e...]
where the time goes in v1:
time: 127 us
  waiting for transfers between devices  44.5 us (35%)
  blocking collectives  29.7 us (23%)
  local copies, waits for them, and re-layouts  18.8 us (15%)
  other arithmetic  15.8 us (12%)
  between operations  14.2 us (11%)
  matrix products  2.29 us (2%)
  starting transfers between devices  1.37 us (1%)
    ppermute x1, waiting for transfers between devices, passed_along(): return lax.ppermute(block, axis, route)  22.3 us
    reduce_scatter x1, waiting for transfers between devices, local(): lax.psum_scatter(jnp.einsum('tbk,tbn->bkn', rows_in, cols_in, preferred_e...  22.1 us
    all_gather x1, blocking collectives, local(): lax.all_gather(own_blocks, 'fsdp', axis=0, tiled=True)  16.1 us
    all_gather x1, blocking collectives, local(): all_indices = lax.all_gather(pattern[0], 'fsdp', axis=0, tiled=True)  13.6 us
    convert_element_type x1, other arithmetic, local(): (hidden_grad.astype(jnp.float32) * silu_slope(pre_act.reshape(tok_rows, -...  8.42 us
    unnamed x5, local copies, waits for them, and re-layouts  7.54 us
    broadcast_in_dim x1, local copies, waits for them, and re-layouts, local(): pre_zero = jnp.zeros((tok_rows, col_count, block_size), jnp.float32)  3.95 us
    scatter-add x1, other arithmetic, forward_step(): return running.at[:, indices[:, 1]].add(product)  3.38 us
  transfers between devices with their start and end apart: 3, of which 2 were waited for; matrix products, arithmetic and copies ran while one was open for 3% of the time, Pallas kernels for 0%

profile of v1, /device:TPU:0, one launch (start us, length us, event | category | flops | bytes accessed | tf_op | source)
XLA Modules:
  0.0 126.6 jit_solution(11105766843554003693)
XLA Ops:
  7.2 0.0 reduce-scatter.2.cloned.1.call-start
  7.2 0.8 copy.12
  8.0 13.6 %all-gather = s32[1,16,2]{2,0,1:T(1,128)S(1)} all-gather(s32[1,4,2]{2,0,1:T(1,128)S(1)} %copy.12), channel_id=2, replica_groups=mesh['section'=2,'fsdp'=4,'dp'=4] {'fsdp'}, dimensions={1}, use_global_device_ids=true | all-gather | bytes 160 | tf_op jit(solution)/shard_map/all_gather | solution.py:46
  21.6 0.1 copy.13
  21.7 1.6 %reshape_squeeze.4 = bf16[128,28,128]{2,1,0:T(8,128)(2,1)S(1)} reshape(bf16[1,4,32,3584]{3,2,1,0:T(8,128)(2,1)} %param.9) | data formatting | bytes 1835008 | tf_op jit(solution)/shard_map/reshape;squeeze | solution.py:43
  23.3 0.4 copy.14
  23.7 16.1 %all-gather.1 = bf16[1,16,128,128]{3,2,0,1:T(8,128)(2,1)S(1)} all-gather(bf16[1,4,128,128]{3,2,0,1:T(8,128)(2,1)} %bitcast.42), channel_id=3, replica_groups=mesh['section'=2,'fsdp'=4,'dp'=4] {'fsdp'}, dimensions={1}, use_global_device_ids=true | all-gather | bytes 655360 | tf_op jit(solution)/shard_map/all_gather | solution.py:77
  39.8 5.9 %copy.20 = f32[16,8,112,128]{3,2,1,0:T(8,128)} copy(bf16[16,8,112,128]{3,1,2,0:T(8,128)(2,1)} %bitcast.39) | data formatting | bytes 11010048
  45.7 0.6 gather_fusion.1
  46.3 0.4 fusion.6
  46.7 3.9 %broadcast_in_dim.44 = f32[128,112,128]{2,0,1:T(8,128)} broadcast(f32[]{:T(128)} %constant.10.clone.1), dimensions={} | broadcast | bytes 7340036 | tf_op jit(solution)/shard_map/broadcast_in_dim | solution.py:56
  50.6 3.4 %scatter_fusion = f32[128,112,128]{2,0,1:T(8,128)} fusion(f32[128,112,128]{2,0,1:T(8,128)} %broadcast_in_dim.44, s32[16]{0:T(128)S(1)} %get-tuple-element.10, f32[16,128,128]{2,1,0:T(8,128)S(1)} %fusion.6), kind=kCustom, calls=%fused_computation.3 | custom fusion | flops 262144 | bytes 3145792 | tf_op jit(solution)/shard_map/scatter-add | solution.py:54
  54.0 8.4 %fusion = bf16[128,112,128]{2,0,1:T(8,128)(2,1)} fusion(f32[128,112,128]{2,1,0:T(8,128)} %bitcast.38, f32[128,112,128]{2,0,1:T(8,128)} %scatter_fusion), kind=kLoop, calls=%fused_computation.6 | loop fusion | flops 16515072 | bytes 18350080 | tf_op jit(solution)/shard_map/convert_element_type | solution.py:60
  62.4 2.7 %gather_fusion.2 = bf16[16,128,128]{2,1,0:T(8,128)(2,1)S(1)} fusion(bf16[128,112,128]{2,0,1:T(8,128)(2,1)} %fusion, s32[1024]{0:T(1024)S(1)} %get-tuple-element.12), kind=kCustom, calls=%fused_computation.1.clone | custom fusion | bytes 1048640 | tf_op jit(solution)/shard_map/jit(_take)/gather | solution.py:67
  65.1 1.4 %fusion.1 = f32[16,128,128]{2,1,0:T(8,128)} fusion(bf16[16,128,128]{2,1,0:T(8,128)(2,1)S(1)} %gather_fusion.1, pred[16]{0:T(512)(128)(4,1)S(1)} %get-tuple-element.8, bf16[16,128,128]{2,1,0:T(8,128)(2,1)S(1)} %gather_fusion.2, pred[16]{0:T(512)(128)(4,1)S(1)} %get-tuple-element.4), kind=kOutput, calls=%fused_computation.8 | convolution fusion | flops 67633152 | bytes 2097184 | tf_op jit(solution)/shard_map/tbk,tbn->bkn/dot_general | solution.py:89
  66.5 0.0 reduce-scatter.2.cloned.1.call-update
  66.6 0.0 all-gather.5.cloned.1.call-start
  66.6 0.5 fusion.3
  67.1 0.2 broadcast_in_dim.43
  67.3 1.6 %scatter_fusion.1 = f32[128,28,128]{2,0,1:T(8,128)S(1)} fusion(f32[128,28,128]{2,0,1:T(8,128)S(1)} %broadcast_in_dim.43, s32[16]{0:T(128)S(1)} %get-tuple-element.11, f32[16,128,128]{2,1,0:T(8,128)S(1)} %fusion.3), kind=kCustom, calls=%fused_computation.4 | custom fusion | flops 262144 | bytes 3145792 | tf_op jit(solution)/shard_map/scatter-add | solution.py:71
  69.0 0.1 convert_element_type.17
  69.1 0.6 copy.17
  69.7 0.5 reshape.36
  70.3 0.6 gather_fusion
  70.9 22.1 %reduce-scatter.2.cloned.1.call-done = f32[4,128,128]{2,1,0:T(8,128)} async-done(((f32[16,128,128]{2,1,0:T(8,128)}), f32[4,128,128]{2,1,0:T(8,128)}) %reduce-scatter.2.cloned.1.call-update) | async-done | bytes 262160 | tf_op jit(solution)/shard_map/reduce_scatter | solution.py:88
  93.0 0.0 all-gather.5.cloned.1.call-update
  93.0 0.2 broadcast_select_fusion
  93.2 1.3 %collective-permute-start = (bf16[4,32,3584]{2,1,0:T(8,128)(2,1)S(1)}, bf16[4,32,3584]{2,1,0:T(8,128)(2,1)S(1)}, u32[]{:S(2)}, u32[]{:S(2)}) collective-permute-start(bf16[4,32,3584]{2,1,0:T(8,128)(2,1)S(1)} %broadcast_select_fusion), channel_id=1, source_target_pairs={{16,0},{17,1},{18,2},{19,3},{20,4},{21,5},{22,6},{23,7},{24,8},{25... | collective-permute-start | bytes 2752520 | tf_op jit(solution)/shard_map/ppermute | solution.py:16
  94.5 22.3 %collective-permute-done = bf16[4,32,3584]{2,1,0:T(8,128)(2,1)S(1)} collective-permute-done((bf16[4,32,3584]{2,1,0:T(8,128)(2,1)S(1)}, bf16[4,32,3584]{2,1,0:T(8,128)(2,1)S(1)}, u32[]{:S(2)}, u32[]{:S(2)}) %collective-permute-start) | collective-permute-done | bytes 917536 | tf_op jit(solution)/shard_map/ppermute | solution.py:16
  116.8 1.3 %reduce_sum.9 = f32[4,128,128]{2,1,0:T(8,128)S(1)} reduce(f32[4,4,128,128]{3,2,1,0:T(8,128)} %bitcast.40, f32[]{:T(128)} %constant.10.clone.1), dimensions={0}, to_apply=%region_3.6 | reduce | flops 196608 | bytes 1310724 | tf_op jit(solution)/shard_map/reduce_sum | solution.py:10
  118.1 0.7 multiply_bitcast_fusion
  118.8 0.9 copy.27
  (9 shorter events, 0.0 us)
Async XLA Ops:
  7.2 85.9 %reduce-scatter.2.cloned.1.call-start = ((), (), s32[]{:S(2)}) async-start(), calls=%async_computation.1 | async-start | bytes 1310720 | tf_op jit(solution)/shard_map/reduce_scatter | solution.py:88
  66.5 3.7 %copy-start = (s32[4]{0:T(128)S(1)}, s32[4]{0:T(128)}, u32[]{:S(2)}) copy-start(s32[4]{0:T(128)} %param.13) | copy-start | bytes 52
  66.6 50.2 %all-gather.5.cloned.1.call-start = ((), (), s32[]{:S(2)}) async-start(), calls=%async_computation.2 | async-start | bytes 1310720 | tf_op jit(solution)/shard_map/all_gather | solution.py:9
  93.2 23.6 %collective-permute-start = (bf16[4,32,3584]{2,1,0:T(8,128)(2,1)S(1)}, bf16[4,32,3584]{2,1,0:T(8,128)(2,1)S(1)}, u32[]{:S(2)}, u32[]{:S(2)}) collective-permute-start(bf16[4,32,3584]{2,1,0:T(8,128)(2,1)S(1)} %broadcast_select_fusion), channel_id=1, source_target_pairs={{16,0},{17,1},{18,2},{19,3},{20,4},{21,5},{22,6},{23,7},{24,8},{25... | collective-permute-start | bytes 2752520 | tf_op jit(solution)/shard_map/ppermute | solution.py:16
Sparse Core Ops, SparseCore 0:
  66.7 26.2 reduce-scatter.1
  94.6 15.1 all-gather.4
